TPU v7x, 512 devices: a whole 4x4x16 slice. The times are simulated.
512 devices in a mesh: ctx: 64 (over z, y_hi, core), head: 8 (over y_lo, x).
Axes of the slice: x: 4, y: 4 (y_hi: 2, y_lo: 2; y = y_hi * 2 + y_lo), z: 16, core: 2. Of those that a mesh axis runs over, the one named last changes fastest.
Arguments:
- query_states: bfloat16 [32768, 8192], P('ctx', 'head'), may hold values from -5 to 5
- key_states: bfloat16 [32768, 1024], P('ctx', 'head'), may hold values from -5 to 5
- value_states: bfloat16 [32768, 1024], P('ctx', 'head'), may hold values from -6 to 6
- out_grad: bfloat16 [32768, 8192], P('ctx', 'head'), may hold values from -6 to 6
- block_lists: int32 [256, 4], replicated, may hold values from 0 to 255, as said below
Outputs:
- query_grad: bfloat16 [32768, 8192], P(('ctx', 'head'))
- key_grad: bfloat16 [32768, 1024], P(('ctx', 'head'))
- value_grad: bfloat16 [32768, 1024], P(('ctx', 'head'))
Inputs may be any that keep to these rules, and one draw needn't show every extreme that they name: `block_lists`: entry 0 of row b is b. The other entries name distinct blocks below b, each held by the same index of ctx as b or by one of the 8 indices just below it; a row with fewer candidates repeats b in its remaining entries. Taken over the 4 rows of one index of ctx, the listed blocks that another index of ctx holds are at most one distinct block.
All inputs are finite; a program needn't handle non-finite values.
Results may differ from a plain program's by a relative error of at most 0.012.
Values may be sent and summed in bfloat16 or wider, within the bound.
No kernel may reach another device: no remote copies, remote signals or barrier semaphores. Data moves between devices by JAX's collectives and lax.ppermute only.
A program may use at most 64 MiB of HBM per device.

v0:
```python
import functools
import math

import jax
import jax.numpy as jnp
from jax import lax
from jax.experimental import pallas as pl
from jax.experimental.pallas import tpu as pltpu
from jax.sharding import PartitionSpec as P


HEAD_DIM = 128
BLOCK = 128
REACH = 8


def from_behind(x, axis, by):
    devices = lax.axis_size(axis)
    pairs = [(i, i + by) for i in range(devices) if 0 <= i + by < devices]
    return lax.ppermute(x, axis, pairs)


def fetch_tree(outgoing):
    step1 = from_behind(outgoing[jnp.array([0, 2, 4, 6])], "ctx", 1)
    step2 = from_behind(jnp.stack([outgoing[1], step1[1], outgoing[5], step1[3]]), "ctx", 2)
    step4 = from_behind(jnp.stack([outgoing[3], step1[2], step2[2], step2[3]]), "ctx", 4)
    step8 = from_behind(outgoing[7], "ctx", 8)
    return jnp.stack([step1[0], step2[0], step2[1], step4[0], step4[1], step4[2], step4[3], step8])


def return_tree(sendback):
    step4 = from_behind(sendback[3:7], "ctx", -4)
    step2 = from_behind(jnp.stack([sendback[1], sendback[2], step4[2], step4[3]]), "ctx", -2)
    step1 = from_behind(jnp.stack([sendback[0], step2[1], step4[1], step2[3]]), "ctx", -1)
    step8 = from_behind(sendback[7], "ctx", -8)
    return jnp.stack([step1[0], step2[0], step1[1], step4[0], step1[2], step2[2], step1[3], step8])


def attn_kernel(slot_ref, use_ref, early_ref, q_ref, g_ref, kv_ref, dq_ref, acc_ref, kv_scr, qs_scr, gs_scr,
                *, chosen, group, scaling):
    n = pl.program_id(0)

    @pl.when(n == 0)
    def _():
        acc_ref[...] = jnp.zeros_like(acc_ref)

    keys = chosen * BLOCK
    for e in range(chosen):
        kv_scr[e * BLOCK:(e + 1) * BLOCK, :] = kv_ref[slot_ref[n * chosen + e]]
    key_cat = kv_scr[:, :HEAD_DIM]
    value_cat = kv_scr[:, HEAD_DIM:]
    for h in range(group):
        qs_scr[h * BLOCK:(h + 1) * BLOCK, :] = q_ref[:, h * HEAD_DIM:(h + 1) * HEAD_DIM]
        gs_scr[h * BLOCK:(h + 1) * BLOCK, :] = g_ref[:, h * HEAD_DIM:(h + 1) * HEAD_DIM]
    q_all = qs_scr[...]
    g_all = gs_scr[...]

    col = lax.broadcasted_iota(jnp.int32, (BLOCK, keys), 1)
    row = lax.broadcasted_iota(jnp.int32, (BLOCK, keys), 0)
    ent = col // BLOCK
    tok = col % BLOCK
    use_col = jnp.zeros((BLOCK, keys), jnp.int32)
    early_col = jnp.zeros((BLOCK, keys), jnp.int32)
    for e in range(chosen):
        use_col = jnp.where(ent == e, use_ref[n * chosen + e], use_col)
        early_col = jnp.where(ent == e, early_ref[n * chosen + e], early_col)
    allowed = (use_col != 0) & ((early_col != 0) | (tok <= row))

    nt = (((1,), (1,)), ((), ()))
    tn = (((0,), (0,)), ((), ()))
    rows = group * BLOCK
    scores = lax.dot_general(q_all, key_cat, nt, preferred_element_type=jnp.float32) * scaling
    scores = scores.reshape(group, BLOCK, keys)
    scores = jnp.where(allowed[None], scores, -1e30)
    row_max = jnp.max(scores, axis=2, keepdims=True)
    total = jnp.sum(jnp.exp(scores - row_max), axis=2, keepdims=True)
    log_total = row_max + jnp.log(total)
    prob = jnp.exp(scores - log_total).reshape(rows, keys)
    prob_half = prob.astype(jnp.bfloat16)
    output = jnp.dot(prob_half, value_cat, preferred_element_type=jnp.float32)
    output = output.astype(jnp.bfloat16).astype(jnp.float32)
    row_dot = jnp.sum(g_all.astype(jnp.float32) * output, axis=1, keepdims=True)
    prob_grad = lax.dot_general(g_all, value_cat, nt, preferred_element_type=jnp.float32)
    score_grad = (prob * (prob_grad - row_dot) * scaling).astype(jnp.bfloat16)
    dq_all = jnp.dot(score_grad, key_cat, preferred_element_type=jnp.float32).astype(jnp.bfloat16)
    for h in range(group):
        dq_ref[:, h * HEAD_DIM:(h + 1) * HEAD_DIM] = dq_all[h * BLOCK:(h + 1) * BLOCK, :]
    key_t = lax.dot_general(q_all, score_grad, tn, preferred_element_type=jnp.float32)
    value_t = lax.dot_general(g_all, prob_half, tn, preferred_element_type=jnp.float32)
    key_part = key_t.T
    value_part = value_t.T

    for e in range(chosen):
        s = slot_ref[n * chosen + e]
        part = slice(e * BLOCK, (e + 1) * BLOCK)
        acc_ref[s, :, :HEAD_DIM] += key_part[part, :]
        acc_ref[s, :, HEAD_DIM:] += value_part[part, :]


def attention_terms(slots, usable, earlier, query_states, out_grad, kv_stock, chosen):
    tok_rows, q_cols = query_states.shape
    slot_count = kv_stock.shape[0]
    group = q_cols // HEAD_DIM
    blocks_here = tok_rows // BLOCK
    kernel = functools.partial(attn_kernel, chosen=chosen, group=group, scaling=1.0 / math.sqrt(HEAD_DIM))
    grid_spec = pltpu.PrefetchScalarGridSpec(
        num_scalar_prefetch=3,
        grid=(blocks_here,),
        in_specs=[
            pl.BlockSpec((BLOCK, q_cols), lambda n, *_: (n, 0)),
            pl.BlockSpec((BLOCK, q_cols), lambda n, *_: (n, 0)),
            pl.BlockSpec((slot_count, BLOCK, 2 * HEAD_DIM), lambda n, *_: (0, 0, 0)),
        ],
        out_specs=[
            pl.BlockSpec((BLOCK, q_cols), lambda n, *_: (n, 0)),
            pl.BlockSpec((slot_count, BLOCK, 2 * HEAD_DIM), lambda n, *_: (0, 0, 0)),
        ],
        scratch_shapes=[
            pltpu.VMEM((chosen * BLOCK, 2 * HEAD_DIM), jnp.bfloat16),
            pltpu.VMEM((group * BLOCK, HEAD_DIM), jnp.bfloat16),
            pltpu.VMEM((group * BLOCK, HEAD_DIM), jnp.bfloat16),
        ],
    )
    return pl.pallas_call(
        kernel,
        grid_spec=grid_spec,
        out_shape=[
            jax.ShapeDtypeStruct((tok_rows, q_cols), jnp.bfloat16),
            jax.ShapeDtypeStruct((slot_count, BLOCK, 2 * HEAD_DIM), jnp.float32),
        ],
        compiler_params=pltpu.CompilerParams(dimension_semantics=("arbitrary",)),
    )(slots, usable, earlier, query_states, out_grad, kv_stock)


def step(query_states, key_states, value_states, out_grad, block_lists):
    ctx_count = lax.axis_size("ctx")
    head_count = lax.axis_size("head")
    myself = lax.axis_index("ctx")
    tok_rows = query_states.shape[0]
    kv_cols = key_states.shape[1]
    blocks_here = tok_rows // BLOCK
    chosen = block_lists.shape[1]
    lists_by_dev = block_lists.reshape(ctx_count, blocks_here * chosen)
    slot_ids = jnp.arange(blocks_here, dtype=jnp.int32)
    distances = jnp.arange(1, REACH + 1, dtype=jnp.int32)
    targets = myself + distances
    target_ok = targets < ctx_count
    target_rows = jnp.take(lists_by_dev, jnp.minimum(targets, ctx_count - 1), axis=0)
    mine = target_rows // blocks_here == myself
    requested = jnp.max(jnp.where(mine, target_rows % blocks_here, -1), axis=1)
    requested = jnp.where(target_ok, requested, -1)
    kv_local = jnp.concatenate([key_states, value_states], axis=1).reshape(blocks_here, BLOCK, 2 * kv_cols)
    outgoing = jnp.take(kv_local, jnp.clip(requested, 0, blocks_here - 1), axis=0)
    kv_stock = jnp.concatenate([kv_local, fetch_tree(outgoing)], axis=0)

    own_entries = lax.dynamic_slice_in_dim(block_lists, myself * blocks_here, blocks_here, 0)
    block_ids = myself * blocks_here + slot_ids
    order_ids = jnp.arange(chosen, dtype=jnp.int32)
    repeat = (own_entries[:, :, None] == own_entries[:, None, :]) & (
        order_ids[None, None, :] < order_ids[None, :, None]
    )
    usable = jnp.logical_not(jnp.any(repeat, axis=2))
    earlier = own_entries < block_ids[:, None]
    behind = myself - own_entries // blocks_here
    slots = jnp.where(behind == 0, own_entries % blocks_here, blocks_here - 1 + behind)
    slots = jnp.clip(slots, 0, blocks_here + REACH - 1)

    query_local, acc = attention_terms(
        slots.reshape(-1).astype(jnp.int32),
        usable.reshape(-1).astype(jnp.int32),
        earlier.reshape(-1).astype(jnp.int32),
        query_states,
        out_grad,
        kv_stock,
        chosen,
    )
    query_grad = lax.all_to_all(query_local, "head", split_axis=0, concat_axis=1, tiled=True)
    sendback = acc[blocks_here:].astype(jnp.bfloat16)
    arrived = return_tree(sendback).astype(jnp.float32)
    credit = (requested[None, :] == slot_ids[:, None]).astype(jnp.float32)
    totals = acc[:blocks_here] + jnp.sum(credit[:, :, None, None] * arrived[None], axis=1)
    kv_grad = totals.reshape(tok_rows, 2 * kv_cols).astype(jnp.bfloat16)
    kv_all = lax.all_to_all(kv_grad, "head", split_axis=0, concat_axis=1, tiled=True)
    out_rows = tok_rows // head_count
    kv_all = kv_all.reshape(out_rows, head_count, 2, kv_cols)
    key_grad = kv_all[:, :, 0, :].reshape(out_rows, head_count * kv_cols)
    value_grad = kv_all[:, :, 1, :].reshape(out_rows, head_count * kv_cols)
    return (query_grad, key_grad, value_grad)


def solution(mesh):
    in_specs = (P("ctx", "head"), P("ctx", "head"), P("ctx", "head"), P("ctx", "head"), P())
    out_specs = (P(("ctx", "head"), None), P(("ctx", "head"), None), P(("ctx", "head"), None))
    return jax.shard_map(step, mesh=mesh, in_specs=in_specs, out_specs=out_specs, check_vma=False)
```

profile of v0, /device:TPU:112, one launch (start us, length us, event | category | flops | bytes accessed | tf_op | source)
XLA Modules:
  0.0 111.4 jit_solution(14127129545167085590)
XLA Ops:
  0.7 0.8 copy.29
  1.5 0.1 reshape.202
  1.6 0.6 gather_fusion
  2.2 0.2 fusion.2
  2.4 1.0 pad_maximum_fusion
  3.4 0.6 gather_fusion.1
  4.0 0.0 copy-start.1
  4.0 0.1 broadcast_select_fusion
  4.1 0.6 gather_fusion.2
  4.7 1.9 %collective-permute-start = (bf16[4,128,256]{2,1,0:T(8,128)(2,1)S(1)}, bf16[4,128,256]{2,1,0:T(8,128)(2,1)S(1)}, u32[]{:S(2)}, u32[]{:S(2)}) collective-permute-start(bf16[4,128,256]{2,1,0:T(8,128)(2,1)S(1)} %gather_fusion.2), channel_id=1, source_target_pairs={{0,8},{8,16},{16,24},{24,32},{32,40},{40,48},{48,56},{56,64},{64,7... | collective-permute-start | bytes 786440 | tf_op jit(solution)/shard_map/ppermute | solution.py:20
  6.7 6.4 %collective-permute-start.3 = (bf16[128,256]{1,0:T(8,128)(2,1)S(1)}, bf16[128,256]{1,0:T(8,128)(2,1)S(1)}, u32[]{:S(2)}, u32[]{:S(2)}) collective-permute-start(bf16[128,256]{1,0:T(8,128)(2,1)S(1)} %get-tuple-element.13), channel_id=1, source_target_pairs={{0,64},{8,72},{16,80},{24,88},{32,96},{40,104},{48,112},{56,120},{... | collective-permute-start | bytes 196616 | tf_op jit(solution)/shard_map/ppermute | solution.py:20
  13.1 0.1 compare_convert_fusion
  13.2 0.7 collective-permute-done
  14.0 6.9 %collective-permute-start.1 = (bf16[4,128,256]{2,1,0:T(8,128)(2,1)S(1)}, bf16[4,128,256]{2,1,0:T(8,128)(2,1)S(1)}, u32[]{:S(2)}, u32[]{:S(2)}) collective-permute-start(bf16[4,128,256]{2,1,0:T(8,128)(2,1)S(1)} %pad_maximum_fusion.1), channel_id=1, source_target_pairs={{0,16},{8,24},{16,32},{24,40},{32,48},{40,56},{48,64},{56,72},{64,... | collective-permute-start | bytes 786440 | tf_op jit(solution)/shard_map/ppermute | solution.py:20
  20.9 0.1 copy.26
  21.0 5.4 %collective-permute-done.1 = bf16[4,128,256]{2,1,0:T(8,128)(2,1)S(1)} collective-permute-done((bf16[4,128,256]{2,1,0:T(8,128)(2,1)S(1)}, bf16[4,128,256]{2,1,0:T(8,128)(2,1)S(1)}, u32[]{:S(2)}, u32[]{:S(2)}) %collective-permute-start.1) | collective-permute-done | bytes 262176 | tf_op jit(solution)/shard_map/ppermute | solution.py:20
  26.4 3.8 %collective-permute-start.2 = (bf16[4,128,256]{2,1,0:T(8,128)(2,1)S(1)}, bf16[4,128,256]{2,1,0:T(8,128)(2,1)S(1)}, u32[]{:S(2)}, u32[]{:S(2)}) collective-permute-start(bf16[4,128,256]{2,1,0:T(8,128)(2,1)S(1)} %pad_maximum_fusion.2), channel_id=1, source_target_pairs={{0,32},{8,40},{16,48},{24,56},{32,64},{40,72},{48,80},{56,88},{64,... | collective-permute-start | bytes 786440 | tf_op jit(solution)/shard_map/ppermute | solution.py:20
  30.3 0.2 and_reduce_fusion
  30.5 0.1 copy.25
  30.6 0.6 reshape.200.slot_ref
  31.2 0.6 reshape.204.use_ref
  31.8 0.1 copy.28
  31.9 0.6 reshape.205.early_ref
  32.5 4.0 %collective-permute-done.2 = bf16[4,128,256]{2,1,0:T(8,128)(2,1)S(1)} collective-permute-done((bf16[4,128,256]{2,1,0:T(8,128)(2,1)S(1)}, bf16[4,128,256]{2,1,0:T(8,128)(2,1)S(1)}, u32[]{:S(2)}, u32[]{:S(2)}) %collective-permute-start.2) | collective-permute-done | bytes 262176 | tf_op jit(solution)/shard_map/ppermute | solution.py:20
  36.6 0.9 copy-done
  37.4 12.8 %shard_map.85 = (bf16[512,1024]{1,0:T(8,128)(2,1)}, f32[12,128,256]{2,1,0:T(8,128)}) custom-call(s32[16]{0:T(128)} %reshape.200.slot_ref, s32[16]{0:T(128)} %reshape.204.use_ref, s32[16]{0:T(128)} %reshape.205.early_ref, bf16[512,1024]{1,0:T(8,128)(2,1)} %q_ref.1, bf16[512,1024]{1,0:T(8,128)(2,1)} %g_ref.1, bf16[12,128,256]{2,1,0:T(8,128)(2,1)} %copy-done), custom_call_target="tpu_custom_call" | custom-call | tf_op jit(solution)/shard_map/pallas_call | solution.py:124
  50.2 1.5 %convert.5 = bf16[12,128,256]{2,1,0:T(8,128)(2,1)S(1)} convert(f32[12,128,256]{2,1,0:T(8,128)} %get-tuple-element.6) | non-fusion elementwise | flops 393216 | bytes 2359296 | tf_op jit(solution)/shard_map/convert.2
  51.8 2.0 %collective-permute-start.4 = (bf16[4,128,256]{2,1,0:T(8,128)(2,1)S(1)}, bf16[4,128,256]{2,1,0:T(8,128)(2,1)S(1)}, u32[]{:S(2)}, u32[]{:S(2)}) collective-permute-start(bf16[4,128,256]{2,1,0:T(8,128)(2,1)S(1)} %slice.149), channel_id=1, source_target_pairs={{32,0},{40,8},{48,16},{56,24},{64,32},{72,40},{80,48},{88,56},{96,... | collective-permute-start | bytes 786440 | tf_op jit(solution)/shard_map/ppermute | solution.py:20
  53.8 8.4 %collective-permute-done.4 = bf16[4,128,256]{2,1,0:T(8,128)(2,1)S(1)} collective-permute-done((bf16[4,128,256]{2,1,0:T(8,128)(2,1)S(1)}, bf16[4,128,256]{2,1,0:T(8,128)(2,1)S(1)}, u32[]{:S(2)}, u32[]{:S(2)}) %collective-permute-start.4) | collective-permute-done | bytes 262176 | tf_op jit(solution)/shard_map/ppermute | solution.py:20
  62.2 4.4 %collective-permute-start.5 = (bf16[4,128,256]{2,1,0:T(8,128)(2,1)S(1)}, bf16[4,128,256]{2,1,0:T(8,128)(2,1)S(1)}, u32[]{:S(2)}, u32[]{:S(2)}) collective-permute-start(bf16[4,128,256]{2,1,0:T(8,128)(2,1)S(1)} %pad_maximum_fusion.3), channel_id=1, source_target_pairs={{16,0},{24,8},{32,16},{40,24},{48,32},{56,40},{64,48},{72,56},{80,... | collective-permute-start | bytes 786440 | tf_op jit(solution)/shard_map/ppermute | solution.py:20
  66.7 7.5 %collective-permute-done.5 = bf16[4,128,256]{2,1,0:T(8,128)(2,1)S(1)} collective-permute-done((bf16[4,128,256]{2,1,0:T(8,128)(2,1)S(1)}, bf16[4,128,256]{2,1,0:T(8,128)(2,1)S(1)}, u32[]{:S(2)}, u32[]{:S(2)}) %collective-permute-start.5) | collective-permute-done | bytes 262176 | tf_op jit(solution)/shard_map/ppermute | solution.py:20
  74.2 1.9 %collective-permute-start.6 = (bf16[4,128,256]{2,1,0:T(8,128)(2,1)S(1)}, bf16[4,128,256]{2,1,0:T(8,128)(2,1)S(1)}, u32[]{:S(2)}, u32[]{:S(2)}) collective-permute-start(bf16[4,128,256]{2,1,0:T(8,128)(2,1)S(1)} %pad_maximum_fusion.4), channel_id=1, source_target_pairs={{8,0},{16,8},{24,16},{32,24},{40,32},{48,40},{56,48},{64,56},{72,6... | collective-permute-start | bytes 786440 | tf_op jit(solution)/shard_map/ppermute | solution.py:20
  76.2 5.8 %all-to-all-start = ((bf16[8,64,1024]{2,1,0:T(8,128)(2,1)}), bf16[8,64,1024]{2,1,0:T(8,128)(2,1)S(1)}, u32[]{:S(2)}, u32[]{:S(2)}) async-start(bf16[8,64,1024]{2,1,0:T(8,128)(2,1)} %bitcast.6), calls=%async_computation | async-start | bytes 2097152 | tf_op jit(solution)/shard_map/all_to_all | solution.py:177
  82.0 1.9 %collective-permute-start.7 = (bf16[128,256]{1,0:T(8,128)(2,1)S(1)}, bf16[128,256]{1,0:T(8,128)(2,1)S(1)}, u32[]{:S(2)}, u32[]{:S(2)}) collective-permute-start(bf16[128,256]{1,0:T(8,128)(2,1)S(1)} %get-tuple-element.11), channel_id=1, source_target_pairs={{64,0},{72,8},{80,16},{88,24},{96,32},{104,40},{112,48},{120,56},{... | collective-permute-start | bytes 196616 | tf_op jit(solution)/shard_map/ppermute | solution.py:20
  84.0 7.4 %collective-permute-done.7 = bf16[128,256]{1,0:T(8,128)(2,1)S(1)} collective-permute-done((bf16[128,256]{1,0:T(8,128)(2,1)S(1)}, bf16[128,256]{1,0:T(8,128)(2,1)S(1)}, u32[]{:S(2)}, u32[]{:S(2)}) %collective-permute-start.7) | collective-permute-done | bytes 65568 | tf_op jit(solution)/shard_map/ppermute | solution.py:20
  91.4 0.1 convert_element_type.37
  91.5 0.4 multiply_reduce_fusion
  91.9 1.8 %add_convert_fusion = bf16[4,128,256]{2,1,0:T(8,128)(2,1)} fusion(f32[4,128,256]{2,1,0:T(8,128)S(1)} %multiply_reduce_fusion, f32[12,128,256]{2,1,0:T(8,128)} %get-tuple-element.6), kind=kLoop, calls=%fused_computation.4 | loop fusion | flops 262144 | bytes 1310720 | tf_op jit(solution)/shard_map/convert_element_type | solution.py:182
  93.7 4.6 %all-to-all-done = bf16[8,64,1024]{2,1,0:T(8,128)(2,1)S(1)} async-done(((bf16[8,64,1024]{2,1,0:T(8,128)(2,1)}), bf16[8,64,1024]{2,1,0:T(8,128)(2,1)S(1)}, u32[]{:S(2)}, u32[]{:S(2)}) %all-to-all-start) | async-done | bytes 1048608 | tf_op jit(solution)/shard_map/all_to_all | solution.py:177
  98.4 3.4 %all-to-all-start.1 = ((bf16[8,64,256]{2,1,0:T(8,128)(2,1)}), bf16[8,64,256]{2,1,0:T(8,128)(2,1)S(1)}, u32[]{:S(2)}, u32[]{:S(2)}) async-start(bf16[8,64,256]{2,1,0:T(8,128)(2,1)} %bitcast.10), calls=%async_computation.1 | async-start | bytes 524288 | tf_op jit(solution)/shard_map/all_to_all | solution.py:183
  101.8 1.1 copy.35
  102.8 6.3 %all-to-all-done.1 = bf16[8,64,256]{2,1,0:T(8,128)(2,1)S(1)} async-done(((bf16[8,64,256]{2,1,0:T(8,128)(2,1)}), bf16[8,64,256]{2,1,0:T(8,128)(2,1)S(1)}, u32[]{:S(2)}, u32[]{:S(2)}) %all-to-all-start.1) | async-done | bytes 262176 | tf_op jit(solution)/shard_map/all_to_all | solution.py:183
  109.2 0.1 reshape.203
  109.2 0.5 fusion.13
  109.7 0.2 copy.33
  109.9 0.7 copy.41
  110.5 0.2 copy.34
  110.7 0.7 copy.40
  (40 shorter events, 0.5 us)
Async XLA Ops:
  4.0 9.1 %copy-start.1 = (s32[256,4]{0,1:T(4,128)S(1)}, s32[256,4]{0,1:T(4,128)}, u32[]{:S(2)}) copy-start(s32[256,4]{0,1:T(4,128)} %param.10) | copy-start | bytes 12292
  4.7 9.2 %collective-permute-start = (bf16[4,128,256]{2,1,0:T(8,128)(2,1)S(1)}, bf16[4,128,256]{2,1,0:T(8,128)(2,1)S(1)}, u32[]{:S(2)}, u32[]{:S(2)}) collective-permute-start(bf16[4,128,256]{2,1,0:T(8,128)(2,1)S(1)} %gather_fusion.2), channel_id=1, source_target_pairs={{0,8},{8,16},{16,24},{24,32},{32,40},{40,48},{48,56},{56,64},{64,7... | collective-permute-start | bytes 786440 | tf_op jit(solution)/shard_map/ppermute | solution.py:20
  6.7 29.9 %collective-permute-start.3 = (bf16[128,256]{1,0:T(8,128)(2,1)S(1)}, bf16[128,256]{1,0:T(8,128)(2,1)S(1)}, u32[]{:S(2)}, u32[]{:S(2)}) collective-permute-start(bf16[128,256]{1,0:T(8,128)(2,1)S(1)} %get-tuple-element.13), channel_id=1, source_target_pairs={{0,64},{8,72},{16,80},{24,88},{32,96},{40,104},{48,112},{56,120},{... | collective-permute-start | bytes 196616 | tf_op jit(solution)/shard_map/ppermute | solution.py:20
  14.0 12.4 %collective-permute-start.1 = (bf16[4,128,256]{2,1,0:T(8,128)(2,1)S(1)}, bf16[4,128,256]{2,1,0:T(8,128)(2,1)S(1)}, u32[]{:S(2)}, u32[]{:S(2)}) collective-permute-start(bf16[4,128,256]{2,1,0:T(8,128)(2,1)S(1)} %pad_maximum_fusion.1), channel_id=1, source_target_pairs={{0,16},{8,24},{16,32},{24,40},{32,48},{40,56},{48,64},{56,72},{64,... | collective-permute-start | bytes 786440 | tf_op jit(solution)/shard_map/ppermute | solution.py:20
  26.4 10.1 %collective-permute-start.2 = (bf16[4,128,256]{2,1,0:T(8,128)(2,1)S(1)}, bf16[4,128,256]{2,1,0:T(8,128)(2,1)S(1)}, u32[]{:S(2)}, u32[]{:S(2)}) collective-permute-start(bf16[4,128,256]{2,1,0:T(8,128)(2,1)S(1)} %pad_maximum_fusion.2), channel_id=1, source_target_pairs={{0,32},{8,40},{16,48},{24,56},{32,64},{40,72},{48,80},{56,88},{64,... | collective-permute-start | bytes 786440 | tf_op jit(solution)/shard_map/ppermute | solution.py:20
  36.6 0.9 copy-start
  51.8 10.4 %collective-permute-start.4 = (bf16[4,128,256]{2,1,0:T(8,128)(2,1)S(1)}, bf16[4,128,256]{2,1,0:T(8,128)(2,1)S(1)}, u32[]{:S(2)}, u32[]{:S(2)}) collective-permute-start(bf16[4,128,256]{2,1,0:T(8,128)(2,1)S(1)} %slice.149), channel_id=1, source_target_pairs={{32,0},{40,8},{48,16},{56,24},{64,32},{72,40},{80,48},{88,56},{96,... | collective-permute-start | bytes 786440 | tf_op jit(solution)/shard_map/ppermute | solution.py:20
  62.2 12.0 %collective-permute-start.5 = (bf16[4,128,256]{2,1,0:T(8,128)(2,1)S(1)}, bf16[4,128,256]{2,1,0:T(8,128)(2,1)S(1)}, u32[]{:S(2)}, u32[]{:S(2)}) collective-permute-start(bf16[4,128,256]{2,1,0:T(8,128)(2,1)S(1)} %pad_maximum_fusion.3), channel_id=1, source_target_pairs={{16,0},{24,8},{32,16},{40,24},{48,32},{56,40},{64,48},{72,56},{80,... | collective-permute-start | bytes 786440 | tf_op jit(solution)/shard_map/ppermute | solution.py:20
  74.2 9.7 %collective-permute-start.6 = (bf16[4,128,256]{2,1,0:T(8,128)(2,1)S(1)}, bf16[4,128,256]{2,1,0:T(8,128)(2,1)S(1)}, u32[]{:S(2)}, u32[]{:S(2)}) collective-permute-start(bf16[4,128,256]{2,1,0:T(8,128)(2,1)S(1)} %pad_maximum_fusion.4), channel_id=1, source_target_pairs={{8,0},{16,8},{24,16},{32,24},{40,32},{48,40},{56,48},{64,56},{72,6... | collective-permute-start | bytes 786440 | tf_op jit(solution)/shard_map/ppermute | solution.py:20
  76.2 22.2 %all-to-all-start = ((bf16[8,64,1024]{2,1,0:T(8,128)(2,1)}), bf16[8,64,1024]{2,1,0:T(8,128)(2,1)S(1)}, u32[]{:S(2)}, u32[]{:S(2)}) async-start(bf16[8,64,1024]{2,1,0:T(8,128)(2,1)} %bitcast.6), calls=%async_computation | async-start | bytes 2097152 | tf_op jit(solution)/shard_map/all_to_all | solution.py:177
  82.0 9.4 %collective-permute-start.7 = (bf16[128,256]{1,0:T(8,128)(2,1)S(1)}, bf16[128,256]{1,0:T(8,128)(2,1)S(1)}, u32[]{:S(2)}, u32[]{:S(2)}) collective-permute-start(bf16[128,256]{1,0:T(8,128)(2,1)S(1)} %get-tuple-element.11), channel_id=1, source_target_pairs={{64,0},{72,8},{80,16},{88,24},{96,32},{104,40},{112,48},{120,56},{... | collective-permute-start | bytes 196616 | tf_op jit(solution)/shard_map/ppermute | solution.py:20
  98.4 10.8 %all-to-all-start.1 = ((bf16[8,64,256]{2,1,0:T(8,128)(2,1)}), bf16[8,64,256]{2,1,0:T(8,128)(2,1)S(1)}, u32[]{:S(2)}, u32[]{:S(2)}) async-start(bf16[8,64,256]{2,1,0:T(8,128)(2,1)} %bitcast.10), calls=%async_computation.1 | async-start | bytes 524288 | tf_op jit(solution)/shard_map/all_to_all | solution.py:183
where the time goes:
time: 112 us; the launch traced here: 111 us
  waiting for transfers between devices  44.3 us (40%)
  starting transfers between devices  38.5 us (34%)
  Pallas kernels  12.8 us (11%)
  local copies, waits for them, and re-layouts  9.06 us (8%)
  other arithmetic  5.61 us (5%)
    ppermute x8, waiting for transfers between devices, from_behind(): return lax.ppermute(x, axis, pairs)  33.4 us
    ppermute x8, starting transfers between devices, from_behind(): return lax.ppermute(x, axis, pairs)  29.3 us
    pallas_call x1, Pallas kernels, attention_terms(): pl.pallas_call(kernel, grid_spec=grid_spec, out_shape=[jax.ShapeDtypeStru...  12.8 us
    all_to_all x1, waiting for transfers between devices, step(): lax.all_to_all(kv_grad, 'head', split_axis=0, concat_axis=1, tiled=True)  6.31 us
    all_to_all x1, starting transfers between devices, step(): lax.all_to_all(query_local, 'head', split_axis=0, concat_axis=1, tiled=True)  5.81 us
    all_to_all x1, waiting for transfers between devices, step(): lax.all_to_all(query_local, 'head', split_axis=0, concat_axis=1, tiled=True)  4.65 us
    unnamed x18, local copies, waits for them, and re-layouts  3.46 us
    all_to_all x1, starting transfers between devices, step(): lax.all_to_all(kv_grad, 'head', split_axis=0, concat_axis=1, tiled=True)  3.41 us
  transfers between devices with their start and end apart: 10, of which 8 were waited for; matrix products, arithmetic and copies ran while one was open for 5% of the time, Pallas kernels for 0%

commit v1 on v0

--- a/solution.py
+++ b/solution.py
@@ -36,9 +36,10 @@
     return jnp.stack([step1[0], step2[0], step1[1], step4[0], step1[2], step2[2], step1[3], step8])
 
 
-def attn_kernel(slot_ref, use_ref, early_ref, q_ref, g_ref, kv_ref, dq_ref, acc_ref, kv_scr, qs_scr, gs_scr,
-                *, chosen, group, scaling):
+def attn_kernel(slot_ref, use_ref, early_ref, q_ref, g_ref, kv_ref, dq_ref, home_ref, away_ref, kv_scr, qs_scr, gs_scr,
+                acc_ref, *, chosen, group, scaling):
     n = pl.program_id(0)
+    homes = home_ref.shape[0]
 
     @pl.when(n == 0)
     def _():
@@ -96,6 +97,11 @@
         acc_ref[s, :, :HEAD_DIM] += key_part[part, :]
         acc_ref[s, :, HEAD_DIM:] += value_part[part, :]
 
+    @pl.when(n == pl.num_programs(0) - 1)
+    def _():
+        home_ref[...] = acc_ref[:homes]
+        away_ref[...] = acc_ref[homes:].astype(jnp.bfloat16)
+
 
 def attention_terms(slots, usable, earlier, query_states, out_grad, kv_stock, chosen):
     tok_rows, q_cols = query_states.shape
@@ -113,12 +119,14 @@
         ],
         out_specs=[
             pl.BlockSpec((BLOCK, q_cols), lambda n, *_: (n, 0)),
-            pl.BlockSpec((slot_count, BLOCK, 2 * HEAD_DIM), lambda n, *_: (0, 0, 0)),
+            pl.BlockSpec((blocks_here, BLOCK, 2 * HEAD_DIM), lambda n, *_: (0, 0, 0)),
+            pl.BlockSpec((slot_count - blocks_here, BLOCK, 2 * HEAD_DIM), lambda n, *_: (0, 0, 0)),
         ],
         scratch_shapes=[
             pltpu.VMEM((chosen * BLOCK, 2 * HEAD_DIM), jnp.bfloat16),
             pltpu.VMEM((group * BLOCK, HEAD_DIM), jnp.bfloat16),
             pltpu.VMEM((group * BLOCK, HEAD_DIM), jnp.bfloat16),
+            pltpu.VMEM((slot_count, BLOCK, 2 * HEAD_DIM), jnp.float32),
         ],
     )
     return pl.pallas_call(
@@ -126,7 +134,8 @@
         grid_spec=grid_spec,
         out_shape=[
             jax.ShapeDtypeStruct((tok_rows, q_cols), jnp.bfloat16),
-            jax.ShapeDtypeStruct((slot_count, BLOCK, 2 * HEAD_DIM), jnp.float32),
+            jax.ShapeDtypeStruct((blocks_here, BLOCK, 2 * HEAD_DIM), jnp.float32),
+            jax.ShapeDtypeStruct((slot_count - blocks_here, BLOCK, 2 * HEAD_DIM), jnp.bfloat16),
         ],
         compiler_params=pltpu.CompilerParams(dimension_semantics=("arbitrary",)),
     )(slots, usable, earlier, query_states, out_grad, kv_stock)
@@ -142,13 +151,11 @@
     chosen = block_lists.shape[1]
     lists_by_dev = block_lists.reshape(ctx_count, blocks_here * chosen)
     slot_ids = jnp.arange(blocks_here, dtype=jnp.int32)
-    distances = jnp.arange(1, REACH + 1, dtype=jnp.int32)
-    targets = myself + distances
-    target_ok = targets < ctx_count
-    target_rows = jnp.take(lists_by_dev, jnp.minimum(targets, ctx_count - 1), axis=0)
+    no_rows = jnp.full((REACH, blocks_here * chosen), -blocks_here, jnp.int32)
+    lists_pad = jnp.concatenate([lists_by_dev, no_rows], axis=0)
+    target_rows = lax.dynamic_slice_in_dim(lists_pad, myself + 1, REACH, 0)
     mine = target_rows // blocks_here == myself
     requested = jnp.max(jnp.where(mine, target_rows % blocks_here, -1), axis=1)
-    requested = jnp.where(target_ok, requested, -1)
     kv_local = jnp.concatenate([key_states, value_states], axis=1).reshape(blocks_here, BLOCK, 2 * kv_cols)
     outgoing = jnp.take(kv_local, jnp.clip(requested, 0, blocks_here - 1), axis=0)
     kv_stock = jnp.concatenate([kv_local, fetch_tree(outgoing)], axis=0)
@@ -165,7 +172,7 @@
     slots = jnp.where(behind == 0, own_entries % blocks_here, blocks_here - 1 + behind)
     slots = jnp.clip(slots, 0, blocks_here + REACH - 1)
 
-    query_local, acc = attention_terms(
+    query_local, home, away = attention_terms(
         slots.reshape(-1).astype(jnp.int32),
         usable.reshape(-1).astype(jnp.int32),
         earlier.reshape(-1).astype(jnp.int32),
@@ -175,10 +182,9 @@
         chosen,
     )
     query_grad = lax.all_to_all(query_local, "head", split_axis=0, concat_axis=1, tiled=True)
-    sendback = acc[blocks_here:].astype(jnp.bfloat16)
-    arrived = return_tree(sendback).astype(jnp.float32)
+    arrived = return_tree(away).astype(jnp.float32)
     credit = (requested[None, :] == slot_ids[:, None]).astype(jnp.float32)
-    totals = acc[:blocks_here] + jnp.sum(credit[:, :, None, None] * arrived[None], axis=1)
+    totals = home + jnp.sum(credit[:, :, None, None] * arrived[None], axis=1)
     kv_grad = totals.reshape(tok_rows, 2 * kv_cols).astype(jnp.bfloat16)
     kv_all = lax.all_to_all(kv_grad, "head", split_axis=0, concat_axis=1, tiled=True)
     out_rows = tok_rows // head_count

time: 112 us -> 111 us (level)
  local copies, waits for them, and re-layouts: 9.06 us -> 11.9 us
  other arithmetic: 5.61 us -> 2.95 us
  waiting for transfers between devices: 44.3 us -> 43 us
    ppermute x8, waiting for transfers between devices: 33.4 us -> 31.6 us  [from_behind(): return lax.ppermute(x, axis, pairs)]
    another operation x1 -> x0, other arithmetic: 1.49 us -> none
    unnamed x18 -> x20, local copies, waits for them, and re-layouts: 3.46 us -> 4.14 us
  transfers between devices with their start and end apart: 10 -> 10, of which waited for: 8 -> 8; matrix products, arithmetic and copies ran while one was open for 5% -> 6% of each run, Pallas kernels for 0% -> 0%
where the time goes in v1:
time: 111 us; the launch traced here: 110 us
  waiting for transfers between devices  43 us (39%)
  starting transfers between devices  38.5 us (35%)
  Pallas kernels  12.8 us (12%)
  local copies, waits for them, and re-layouts  11.9 us (11%)
  other arithmetic  2.95 us (3%)
    ppermute x8, waiting for transfers between devices, from_behind(): return lax.ppermute(x, axis, pairs)  31.6 us
    ppermute x8, starting transfers between devices, from_behind(): return lax.ppermute(x, axis, pairs)  29.3 us
    pallas_call x1, Pallas kernels, attention_terms(): pl.pallas_call(kernel, grid_spec=grid_spec, out_shape=[jax.ShapeDtypeStru...  12.8 us
    all_to_all x1, waiting for transfers between devices, step(): lax.all_to_all(kv_grad, 'head', split_axis=0, concat_axis=1, tiled=True)  6.31 us
    all_to_all x1, starting transfers between devices, step(): lax.all_to_all(query_local, 'head', split_axis=0, concat_axis=1, tiled=True)  5.8 us
    all_to_all x1, waiting for transfers between devices, step(): lax.all_to_all(query_local, 'head', split_axis=0, concat_axis=1, tiled=True)  5.04 us
    unnamed x20, local copies, waits for them, and re-layouts  4.14 us
    all_to_all x1, starting transfers between devices, step(): lax.all_to_all(kv_grad, 'head', split_axis=0, concat_axis=1, tiled=True)  3.41 us
  transfers between devices with their start and end apart: 10, of which 8 were waited for; matrix products, arithmetic and copies ran while one was open for 6% of the time, Pallas kernels for 0%

profile of v1, /device:TPU:112, one launch (start us, length us, event | category | flops | bytes accessed | tf_op | source)
XLA Modules:
  0.0 110.2 jit_solution(7435925576125187313)
XLA Ops:
  0.6 0.8 copy.28
  1.5 0.1 reshape.160
  1.6 0.1 fusion.2
  1.7 1.0 pad_maximum_fusion
  2.8 0.6 gather_fusion
  3.3 0.1 broadcast_select_fusion
  3.5 0.6 gather_fusion.1
  4.0 1.9 %collective-permute-start = (bf16[4,128,256]{2,1,0:T(8,128)(2,1)S(1)}, bf16[4,128,256]{2,1,0:T(8,128)(2,1)S(1)}, u32[]{:S(2)}, u32[]{:S(2)}) collective-permute-start(bf16[4,128,256]{2,1,0:T(8,128)(2,1)S(1)} %gather_fusion.1), channel_id=1, source_target_pairs={{0,8},{8,16},{16,24},{24,32},{32,40},{40,48},{48,56},{56,64},{64,7... | collective-permute-start | bytes 786440 | tf_op jit(solution)/shard_map/ppermute | solution.py:20
  6.0 6.4 %collective-permute-start.3 = (bf16[128,256]{1,0:T(8,128)(2,1)S(1)}, bf16[128,256]{1,0:T(8,128)(2,1)S(1)}, u32[]{:S(2)}, u32[]{:S(2)}) collective-permute-start(bf16[128,256]{1,0:T(8,128)(2,1)S(1)} %get-tuple-element.13), channel_id=1, source_target_pairs={{0,64},{8,72},{16,80},{24,88},{32,96},{40,104},{48,112},{56,120},{... | collective-permute-start | bytes 196616 | tf_op jit(solution)/shard_map/ppermute | solution.py:20
  12.4 0.1 compare_convert_fusion
  12.5 0.7 collective-permute-done
  13.3 6.9 %collective-permute-start.1 = (bf16[4,128,256]{2,1,0:T(8,128)(2,1)S(1)}, bf16[4,128,256]{2,1,0:T(8,128)(2,1)S(1)}, u32[]{:S(2)}, u32[]{:S(2)}) collective-permute-start(bf16[4,128,256]{2,1,0:T(8,128)(2,1)S(1)} %pad_maximum_fusion.1), channel_id=1, source_target_pairs={{0,16},{8,24},{16,32},{24,40},{32,48},{40,56},{48,64},{56,72},{64,... | collective-permute-start | bytes 786440 | tf_op jit(solution)/shard_map/ppermute | solution.py:20
  20.2 0.1 copy.25
  20.4 5.4 %collective-permute-done.1 = bf16[4,128,256]{2,1,0:T(8,128)(2,1)S(1)} collective-permute-done((bf16[4,128,256]{2,1,0:T(8,128)(2,1)S(1)}, bf16[4,128,256]{2,1,0:T(8,128)(2,1)S(1)}, u32[]{:S(2)}, u32[]{:S(2)}) %collective-permute-start.1) | collective-permute-done | bytes 262176 | tf_op jit(solution)/shard_map/ppermute | solution.py:20
  25.8 3.8 %collective-permute-start.2 = (bf16[4,128,256]{2,1,0:T(8,128)(2,1)S(1)}, bf16[4,128,256]{2,1,0:T(8,128)(2,1)S(1)}, u32[]{:S(2)}, u32[]{:S(2)}) collective-permute-start(bf16[4,128,256]{2,1,0:T(8,128)(2,1)S(1)} %pad_maximum_fusion.2), channel_id=1, source_target_pairs={{0,32},{8,40},{16,48},{24,56},{32,64},{40,72},{48,80},{56,88},{64,... | collective-permute-start | bytes 786440 | tf_op jit(solution)/shard_map/ppermute | solution.py:20
  29.6 0.2 and_reduce_fusion
  29.8 0.1 copy.24
  29.9 0.6 reshape.158.slot_ref
  30.5 0.6 reshape.162.use_ref
  31.1 0.1 copy.27
  31.2 0.6 reshape.163.early_ref
  31.8 4.0 %collective-permute-done.2 = bf16[4,128,256]{2,1,0:T(8,128)(2,1)S(1)} collective-permute-done((bf16[4,128,256]{2,1,0:T(8,128)(2,1)S(1)}, bf16[4,128,256]{2,1,0:T(8,128)(2,1)S(1)}, u32[]{:S(2)}, u32[]{:S(2)}) %collective-permute-start.2) | collective-permute-done | bytes 262176 | tf_op jit(solution)/shard_map/ppermute | solution.py:20
  35.9 0.9 copy-done
  36.8 12.8 %shard_map.85 = (bf16[512,1024]{1,0:T(8,128)(2,1)}, f32[4,128,256]{2,1,0:T(8,128)}, bf16[8,128,256]{2,1,0:T(8,128)(2,1)}) custom-call(s32[16]{0:T(128)} %reshape.158.slot_ref, s32[16]{0:T(128)} %reshape.162.use_ref, s32[16]{0:T(128)} %reshape.163.early_ref, bf16[512,1024]{1,0:T(8,128)(2,1)} %q_ref.1, bf16[512,1024]{1,0:T(8,128)(2,1)} %g_ref.1, ...), custom_call_target="tpu_custom_call" | custom-call | tf_op jit(solution)/shard_map/pallas_call | solution.py:132
  49.6 1.0 slice.106
  50.6 2.0 %collective-permute-start.4 = (bf16[4,128,256]{2,1,0:T(8,128)(2,1)S(1)}, bf16[4,128,256]{2,1,0:T(8,128)(2,1)S(1)}, u32[]{:S(2)}, u32[]{:S(2)}) collective-permute-start(bf16[4,128,256]{2,1,0:T(8,128)(2,1)S(1)} %slice.106), channel_id=1, source_target_pairs={{32,0},{40,8},{48,16},{56,24},{64,32},{72,40},{80,48},{88,56},{96,... | collective-permute-start | bytes 786440 | tf_op jit(solution)/shard_map/ppermute | solution.py:20
  52.6 0.9 slice.105
  53.5 7.5 %collective-permute-done.4 = bf16[4,128,256]{2,1,0:T(8,128)(2,1)S(1)} collective-permute-done((bf16[4,128,256]{2,1,0:T(8,128)(2,1)S(1)}, bf16[4,128,256]{2,1,0:T(8,128)(2,1)S(1)}, u32[]{:S(2)}, u32[]{:S(2)}) %collective-permute-start.4) | collective-permute-done | bytes 262176 | tf_op jit(solution)/shard_map/ppermute | solution.py:20
  61.1 4.4 %collective-permute-start.5 = (bf16[4,128,256]{2,1,0:T(8,128)(2,1)S(1)}, bf16[4,128,256]{2,1,0:T(8,128)(2,1)S(1)}, u32[]{:S(2)}, u32[]{:S(2)}) collective-permute-start(bf16[4,128,256]{2,1,0:T(8,128)(2,1)S(1)} %pad_maximum_fusion.3), channel_id=1, source_target_pairs={{16,0},{24,8},{32,16},{40,24},{48,32},{56,40},{64,48},{72,56},{80,... | collective-permute-start | bytes 786440 | tf_op jit(solution)/shard_map/ppermute | solution.py:20
  65.4 0.9 slice_bitcast_fusion.1
  66.3 6.7 %collective-permute-done.5 = bf16[4,128,256]{2,1,0:T(8,128)(2,1)S(1)} collective-permute-done((bf16[4,128,256]{2,1,0:T(8,128)(2,1)S(1)}, bf16[4,128,256]{2,1,0:T(8,128)(2,1)S(1)}, u32[]{:S(2)}, u32[]{:S(2)}) %collective-permute-start.5) | collective-permute-done | bytes 262176 | tf_op jit(solution)/shard_map/ppermute | solution.py:20
  73.1 1.9 %collective-permute-start.6 = (bf16[4,128,256]{2,1,0:T(8,128)(2,1)S(1)}, bf16[4,128,256]{2,1,0:T(8,128)(2,1)S(1)}, u32[]{:S(2)}, u32[]{:S(2)}) collective-permute-start(bf16[4,128,256]{2,1,0:T(8,128)(2,1)S(1)} %pad_maximum_fusion.4), channel_id=1, source_target_pairs={{8,0},{16,8},{24,16},{32,24},{40,32},{48,40},{56,48},{64,56},{72,6... | collective-permute-start | bytes 786440 | tf_op jit(solution)/shard_map/ppermute | solution.py:20
  75.0 5.8 %all-to-all-start = ((bf16[8,64,1024]{2,1,0:T(8,128)(2,1)}), bf16[8,64,1024]{2,1,0:T(8,128)(2,1)S(1)}, u32[]{:S(2)}, u32[]{:S(2)}) async-start(bf16[8,64,1024]{2,1,0:T(8,128)(2,1)} %bitcast.5), calls=%async_computation | async-start | bytes 2097152 | tf_op jit(solution)/shard_map/all_to_all | solution.py:184
  80.8 1.9 %collective-permute-start.7 = (bf16[128,256]{1,0:T(8,128)(2,1)S(1)}, bf16[128,256]{1,0:T(8,128)(2,1)S(1)}, u32[]{:S(2)}, u32[]{:S(2)}) collective-permute-start(bf16[128,256]{1,0:T(8,128)(2,1)S(1)} %get-tuple-element.11), channel_id=1, source_target_pairs={{64,0},{72,8},{80,16},{88,24},{96,32},{104,40},{112,48},{120,56},{... | collective-permute-start | bytes 196616 | tf_op jit(solution)/shard_map/ppermute | solution.py:20
  82.8 7.4 %collective-permute-done.7 = bf16[128,256]{1,0:T(8,128)(2,1)S(1)} collective-permute-done((bf16[128,256]{1,0:T(8,128)(2,1)S(1)}, bf16[128,256]{1,0:T(8,128)(2,1)S(1)}, u32[]{:S(2)}, u32[]{:S(2)}) %collective-permute-start.7) | collective-permute-done | bytes 65568 | tf_op jit(solution)/shard_map/ppermute | solution.py:20
  90.2 0.1 convert_element_type.36
  90.3 0.4 multiply_reduce_fusion
  90.7 0.7 copy-done.1
  91.4 0.8 add_convert_fusion
  92.1 5.0 %all-to-all-done = bf16[8,64,1024]{2,1,0:T(8,128)(2,1)S(1)} async-done(((bf16[8,64,1024]{2,1,0:T(8,128)(2,1)}), bf16[8,64,1024]{2,1,0:T(8,128)(2,1)S(1)}, u32[]{:S(2)}, u32[]{:S(2)}) %all-to-all-start) | async-done | bytes 1048608 | tf_op jit(solution)/shard_map/all_to_all | solution.py:184
  97.2 3.4 %all-to-all-start.1 = ((bf16[8,64,256]{2,1,0:T(8,128)(2,1)}), bf16[8,64,256]{2,1,0:T(8,128)(2,1)S(1)}, u32[]{:S(2)}, u32[]{:S(2)}) async-start(bf16[8,64,256]{2,1,0:T(8,128)(2,1)} %bitcast.9), calls=%async_computation.1 | async-start | bytes 524288 | tf_op jit(solution)/shard_map/all_to_all | solution.py:189
  100.6 1.1 copy.34
  101.7 6.3 %all-to-all-done.1 = bf16[8,64,256]{2,1,0:T(8,128)(2,1)S(1)} async-done(((bf16[8,64,256]{2,1,0:T(8,128)(2,1)}), bf16[8,64,256]{2,1,0:T(8,128)(2,1)S(1)}, u32[]{:S(2)}, u32[]{:S(2)}) %all-to-all-start.1) | async-done | bytes 262176 | tf_op jit(solution)/shard_map/all_to_all | solution.py:189
  108.0 0.5 fusion.11
  108.5 0.2 copy.32
  108.7 0.7 copy.40
  109.4 0.2 copy.33
  109.5 0.7 copy.39
  (37 shorter events, 0.5 us)
Async XLA Ops:
  3.5 9.0 %copy-start.2 = (s32[256,4]{0,1:T(4,128)S(1)}, s32[256,4]{0,1:T(4,128)}, u32[]{:S(2)}) copy-start(s32[256,4]{0,1:T(4,128)} %param.10) | copy-start | bytes 12292
  4.0 9.2 %collective-permute-start = (bf16[4,128,256]{2,1,0:T(8,128)(2,1)S(1)}, bf16[4,128,256]{2,1,0:T(8,128)(2,1)S(1)}, u32[]{:S(2)}, u32[]{:S(2)}) collective-permute-start(bf16[4,128,256]{2,1,0:T(8,128)(2,1)S(1)} %gather_fusion.1), channel_id=1, source_target_pairs={{0,8},{8,16},{16,24},{24,32},{32,40},{40,48},{48,56},{56,64},{64,7... | collective-permute-start | bytes 786440 | tf_op jit(solution)/shard_map/ppermute | solution.py:20
  6.0 29.9 %collective-permute-start.3 = (bf16[128,256]{1,0:T(8,128)(2,1)S(1)}, bf16[128,256]{1,0:T(8,128)(2,1)S(1)}, u32[]{:S(2)}, u32[]{:S(2)}) collective-permute-start(bf16[128,256]{1,0:T(8,128)(2,1)S(1)} %get-tuple-element.13), channel_id=1, source_target_pairs={{0,64},{8,72},{16,80},{24,88},{32,96},{40,104},{48,112},{56,120},{... | collective-permute-start | bytes 196616 | tf_op jit(solution)/shard_map/ppermute | solution.py:20
  13.3 12.4 %collective-permute-start.1 = (bf16[4,128,256]{2,1,0:T(8,128)(2,1)S(1)}, bf16[4,128,256]{2,1,0:T(8,128)(2,1)S(1)}, u32[]{:S(2)}, u32[]{:S(2)}) collective-permute-start(bf16[4,128,256]{2,1,0:T(8,128)(2,1)S(1)} %pad_maximum_fusion.1), channel_id=1, source_target_pairs={{0,16},{8,24},{16,32},{24,40},{32,48},{40,56},{48,64},{56,72},{64,... | collective-permute-start | bytes 786440 | tf_op jit(solution)/shard_map/ppermute | solution.py:20
  25.8 10.1 %collective-permute-start.2 = (bf16[4,128,256]{2,1,0:T(8,128)(2,1)S(1)}, bf16[4,128,256]{2,1,0:T(8,128)(2,1)S(1)}, u32[]{:S(2)}, u32[]{:S(2)}) collective-permute-start(bf16[4,128,256]{2,1,0:T(8,128)(2,1)S(1)} %pad_maximum_fusion.2), channel_id=1, source_target_pairs={{0,32},{8,40},{16,48},{24,56},{32,64},{40,72},{48,80},{56,88},{64,... | collective-permute-start | bytes 786440 | tf_op jit(solution)/shard_map/ppermute | solution.py:20
  35.9 0.9 copy-start
  50.6 10.4 %collective-permute-start.4 = (bf16[4,128,256]{2,1,0:T(8,128)(2,1)S(1)}, bf16[4,128,256]{2,1,0:T(8,128)(2,1)S(1)}, u32[]{:S(2)}, u32[]{:S(2)}) collective-permute-start(bf16[4,128,256]{2,1,0:T(8,128)(2,1)S(1)} %slice.106), channel_id=1, source_target_pairs={{32,0},{40,8},{48,16},{56,24},{64,32},{72,40},{80,48},{88,56},{96,... | collective-permute-start | bytes 786440 | tf_op jit(solution)/shard_map/ppermute | solution.py:20
  61.1 12.0 %collective-permute-start.5 = (bf16[4,128,256]{2,1,0:T(8,128)(2,1)S(1)}, bf16[4,128,256]{2,1,0:T(8,128)(2,1)S(1)}, u32[]{:S(2)}, u32[]{:S(2)}) collective-permute-start(bf16[4,128,256]{2,1,0:T(8,128)(2,1)S(1)} %pad_maximum_fusion.3), channel_id=1, source_target_pairs={{16,0},{24,8},{32,16},{40,24},{48,32},{56,40},{64,48},{72,56},{80,... | collective-permute-start | bytes 786440 | tf_op jit(solution)/shard_map/ppermute | solution.py:20
  73.1 9.7 %collective-permute-start.6 = (bf16[4,128,256]{2,1,0:T(8,128)(2,1)S(1)}, bf16[4,128,256]{2,1,0:T(8,128)(2,1)S(1)}, u32[]{:S(2)}, u32[]{:S(2)}) collective-permute-start(bf16[4,128,256]{2,1,0:T(8,128)(2,1)S(1)} %pad_maximum_fusion.4), channel_id=1, source_target_pairs={{8,0},{16,8},{24,16},{32,24},{40,32},{48,40},{56,48},{64,56},{72,6... | collective-permute-start | bytes 786440 | tf_op jit(solution)/shard_map/ppermute | solution.py:20
  75.0 22.2 %all-to-all-start = ((bf16[8,64,1024]{2,1,0:T(8,128)(2,1)}), bf16[8,64,1024]{2,1,0:T(8,128)(2,1)S(1)}, u32[]{:S(2)}, u32[]{:S(2)}) async-start(bf16[8,64,1024]{2,1,0:T(8,128)(2,1)} %bitcast.5), calls=%async_computation | async-start | bytes 2097152 | tf_op jit(solution)/shard_map/all_to_all | solution.py:184
  80.8 9.4 %collective-permute-start.7 = (bf16[128,256]{1,0:T(8,128)(2,1)S(1)}, bf16[128,256]{1,0:T(8,128)(2,1)S(1)}, u32[]{:S(2)}, u32[]{:S(2)}) collective-permute-start(bf16[128,256]{1,0:T(8,128)(2,1)S(1)} %get-tuple-element.11), channel_id=1, source_target_pairs={{64,0},{72,8},{80,16},{88,24},{96,32},{104,40},{112,48},{120,56},{... | collective-permute-start | bytes 196616 | tf_op jit(solution)/shard_map/ppermute | solution.py:20
  90.3 1.0 copy-start.1
  97.2 10.8 %all-to-all-start.1 = ((bf16[8,64,256]{2,1,0:T(8,128)(2,1)}), bf16[8,64,256]{2,1,0:T(8,128)(2,1)S(1)}, u32[]{:S(2)}, u32[]{:S(2)}) async-start(bf16[8,64,256]{2,1,0:T(8,128)(2,1)} %bitcast.9), calls=%async_computation.1 | async-start | bytes 524288 | tf_op jit(solution)/shard_map/all_to_all | solution.py:189
